TPU v7x, 256 devices: a whole 4x4x8 slice. The times are simulated.
256 devices in a mesh: dp: 32 (over z, y_hi, core), inner: 8 (over y_lo, x).
Axes of the slice: x: 4, y: 4 (y_hi: 2, y_lo: 2; y = y_hi * 2 + y_lo), z: 8, core: 2. Of those that a mesh axis runs over, the one named last changes fastest.
Arguments:
- tokens: bfloat16 [131072, 1664], P(('dp', 'inner')), may hold values from -16 to 16
- attn_gain: float32 [1664], replicated, may hold values from 0.1 to 1.9
- qkv_weight: bfloat16 [3, 1664, 832], P(None, 'dp', 'inner'), may hold values from -6 to 6
- out_weight: bfloat16 [832, 1664], P('inner', 'dp'), may hold values from -0.21875 to 0.21875
- merge_gain: float32 [6656], replicated, may hold values from 0.25 to 1.75
- merge_weight: bfloat16 [6656, 2048], P('dp', 'inner'), may hold values from -0.078125 to 0.078125
- segment_ids: int32 [131072], P('dp'), may hold values from -1 to 7, as said below
- owners: int32 [32768, 1], P('dp'), may hold values from 0 to 31; in each aligned block of 1024 rows (0 to 1023, 1024 to 2047, ...) at most 64 rows name the same one
Outputs:
- merged_out: bfloat16 [65536, 2048], P('dp', 'inner')
Inputs may be any that keep to these rules, and one draw needn't show every extreme that they name: `segment_ids`: within each device's aligned block of 512 tokens, ids never fall except to -1, which fills a tail of 4 or more tokens; every run of one id starts at a multiple of 4 and holds a multiple of 4 tokens. `owners`: in each aligned block of 1024 rows (the rows of one index of dp) no owner is named by more than 64 rows.
All inputs are finite; a program needn't handle non-finite values.
Results may differ from a plain program's by a relative error of at most 0.0062.
Values may be sent and summed in bfloat16 or wider, within the bound.
No kernel may reach another device: no remote copies, remote signals or barrier semaphores. Data moves between devices by JAX's collectives and lax.ppermute only.
A program may use at most 128 MiB of HBM per device.

v0:
```python
import jax
import jax.numpy as jnp
from jax import lax
from jax.sharding import PartitionSpec as P

HEAD_DIM = 104
EPS = 1e-06
NEG = -1e30


def layer_norm(values, gain):
    values = values.astype(jnp.float32)
    center = values - jnp.mean(values, axis=-1, keepdims=True)
    spread = jnp.mean(center * center, axis=-1, keepdims=True)
    return center * lax.rsqrt(spread + EPS) * gain


def attend_block(queries, keys, vectors, segment):
    scale = queries.shape[-1] ** (-0.5)
    scores = jnp.einsum("qhe,khe->hqk", queries, keys, preferred_element_type=jnp.float32) * scale
    visible = segment[:, None] == segment[None, :]
    scores = jnp.where(visible[None, :, :], scores, NEG)
    top = jnp.max(scores, axis=-1, keepdims=True)
    weights = jnp.exp(scores - top)
    probs = (weights / jnp.sum(weights, axis=-1, keepdims=True)).astype(jnp.bfloat16)
    context = jnp.einsum("hqk,khe->qhe", probs, vectors, preferred_element_type=jnp.float32)
    return context.astype(jnp.bfloat16)


def split_heads(projected):
    shaped = projected.reshape(3, projected.shape[1], projected.shape[2] // HEAD_DIM, HEAD_DIM)
    return (shaped[0], shaped[1], shaped[2])


def local(tokens, attn_gain, qkv_weight, out_weight, merge_gain, merge_weight, segment_ids, owners):
    tok_rows = tokens.shape[0]
    local_segment = lax.dynamic_slice_in_dim(
        segment_ids, lax.axis_index("inner") * tok_rows, tok_rows
    )
    normed = layer_norm(tokens, attn_gain).astype(jnp.bfloat16)
    qkv_part = lax.all_gather(qkv_weight, "inner", axis=2, tiled=True)
    projected = jnp.einsum(
        "td,cdh->cth",
        normed,
        lax.all_gather(qkv_part, "dp", axis=1, tiled=True),
        preferred_element_type=jnp.float32,
    )
    queries, keys, vectors = split_heads(projected.astype(jnp.bfloat16))
    context = attend_block(queries, keys, vectors, local_segment).reshape(tok_rows, -1)
    out_part = lax.all_gather(out_weight, "inner", axis=0, tiled=True)
    attn_out = jnp.dot(
        context,
        lax.all_gather(out_part, "dp", axis=1, tiled=True),
        preferred_element_type=jnp.float32,
    )
    hidden = tokens.astype(jnp.float32) + attn_out
    quad_rows = hidden.reshape(tok_rows // 4, -1)
    live = local_segment.reshape(-1, 4)[:, 0] >= 0
    merged = jnp.where(live[:, None], layer_norm(quad_rows, merge_gain), 0.0).astype(jnp.bfloat16)
    merge_full = lax.all_gather(merge_weight, "dp", axis=0, tiled=True)
    features = jnp.dot(
        lax.all_gather(merged, "inner", axis=0, tiled=True),
        merge_full,
        preferred_element_type=jnp.float32,
    ).astype(jnp.bfloat16)
    n_dp = lax.axis_size("dp")
    group_rows = features.shape[0]
    slots = 2 * group_rows // n_dp
    owner_col = owners[:, 0]
    chosen = (owner_col[:, None] == jnp.arange(n_dp, dtype=jnp.int32)[None, :]).astype(jnp.int32)
    earlier = jnp.cumsum(chosen, axis=0) - chosen
    rank = jnp.sum(earlier * chosen, axis=1)
    target = owner_col * slots + rank
    source_row = (
        jnp.full((n_dp * slots,), group_rows, jnp.int32)
        .at[target]
        .set(jnp.arange(group_rows, dtype=jnp.int32))
    )
    padded = jnp.concatenate([features, jnp.zeros((1, features.shape[1]), jnp.bfloat16)], axis=0)
    outgoing = padded[source_row]
    return lax.all_to_all(outgoing, "dp", split_axis=0, concat_axis=0, tiled=True)


def solution(mesh):
    placed = (
        P(("dp", "inner"), None),
        P(),
        P(None, "dp", "inner"),
        P("inner", "dp"),
        P(),
        P("dp", "inner"),
        P("dp"),
        P("dp", None),
    )
    return jax.shard_map(
        local, mesh=mesh, in_specs=placed, out_specs=P("dp", "inner"), check_vma=False
    )
```

profile of v0, /device:TPU:1, one launch (start us, length us, event | category | flops | bytes accessed | tf_op | source)
XLA Modules:
  0.0 524.1 jit_solution(5814935744648838367)
XLA Ops:
  6.5 23.5 %all-gather = bf16[8,104,52]{1,2,0:T(8,128)(2,1)S(1)} all-gather(bf16[1,104,52]{1,2,0:T(8,128)(2,1)} %bitcast.61), channel_id=1, replica_groups=mesh['dp'=32,'inner'=8] {'inner'}, dimensions={0}, use_global_device_ids=true | all-gather | bytes 97344 | tf_op jit(solution)/shard_map/all_gather | solution.py:50
  30.9 0.9 copy.18
  31.8 24.0 %all_gather.18 = bf16[3,52,832]{1,0,2:T(4,128)(2,1)S(1)} all-gather(bf16[3,52,104]{1,0,2:T(4,128)(2,1)S(1)} %copy.18), channel_id=1, replica_groups=mesh['dp'=32,'inner'=8] {'inner'}, dimensions={2}, use_global_device_ids=true | all-gather | bytes 292032 | tf_op jit(solution)/shard_map/all_gather | solution.py:41
  55.8 1.7 copy.19
  60.3 0.9 broadcast_compare_fusion
  61.2 62.0 %all-gather.13.cloned.1.call-done = bf16[32,52,832]{2,1,0:T(8,128)(2,1)} async-done(((bf16[1,52,832]{2,1,0:T(8,128)(2,1)}), bf16[32,52,832]{2,1,0:T(8,128)(2,1)}) %all-gather.13.cloned.1.call-update) | async-done | bytes 2768912 | tf_op jit(solution)/shard_map/all_gather | solution.py:53
  123.2 5.6 %reshape.117 = bf16[1664,832]{1,0:T(8,128)(2,1)} reshape(bf16[32,52,832]{2,1,0:T(8,128)(2,1)} %all-gather.13.cloned.1.call-done) | data formatting | bytes 5537792
  128.8 108.2 %all-gather.7.cloned.1.call-done = bf16[3,1664,832]{2,0,1:T(4,128)(2,1)} async-done(((bf16[3,52,832]{2,0,1:T(4,128)(2,1)}), bf16[3,1664,832]{2,0,1:T(4,128)(2,1)}) %all-gather.7.cloned.1.call-update) | async-done | bytes 8306704 | tf_op jit(solution)/shard_map/all_gather | solution.py:45
  237.0 12.2 %convert_bitcast_fusion = bf16[3,512,832]{1,2,0:T(8,128)(2,1)S(1)} fusion(bf16[3,1664,832]{2,0,1:T(4,128)(2,1)} %all-gather.7.cloned.1.call-done, bf16[512,1664]{1,0:T(8,128)(2,1)S(1)} %copy-done, f32[1664]{0:T(1024)S(1)} %copy-done.4, f32[512]{0:T(512)S(1)} %add_rsqrt_fusion, f32[512]{0:T(512)S(1)} %broadcast_multiply_fusion), kind=kOutput, calls=%fused_computation.23 | convolution fusion | flops 4258562048 | bytes 12577280 | tf_op jit(solution)/shard_map/td,cdh->cth/dot_general | solution.py:42
  249.2 1.1 fusion.33
  250.3 7.8 %fusion.34 = (f32[8,512]{1,0:T(8,128)S(1)}, f32[8,512,512]{1,2,0:T(8,128)}) fusion(pred[512,512]{0,1:T(8,128)(4,1)} %broadcast_compare_fusion, bf16[512,8,104]{0,2,1:T(8,128)(2,1)} %bitcast.54, bf16[512,8,104]{0,2,1:T(8,128)(2,1)S(1)} %bitcast.53), kind=kOutput, calls=%fused_computation.54 | convolution fusion | flops 444596736 | bytes 10371072 | tf_op jit(solution)/shard_map/sub | solution.py:24
  258.1 4.3 fusion.20
  262.4 3.9 fusion.35
  266.7 2.9 reshape.95
  269.7 2.4 multiply_reduce_fusion
  272.4 1.8 select_convert_fusion
  274.2 9.2 %reduce-window.6 = s32[32,8,128]{2,1,0:T(8,128)S(1)} reduce-window(s32[32,8,128]{2,1,0:T(8,128)S(1)} %fusion.26, s32[]{:T(128)} %constant.18.clone.1), window={size=1x1x128 pad=0_0x0_0x127_0}, to_apply=%region_8.9 | reduce-window | flops 4161536 | bytes 262148 | tf_op jit(solution)/shard_map/reduce-window
  284.0 4.3 scatter_custom_fusion
  288.3 32.0 %all-gather.11.cloned.1.call-done = bf16[6656,256]{1,0:T(8,128)(2,1)} async-done(((bf16[208,256]{1,0:T(8,128)(2,1)}), bf16[6656,256]{1,0:T(8,128)(2,1)}) %all-gather.11.cloned.1.call-update) | async-done | bytes 3407888 | tf_op jit(solution)/shard_map/all_gather | solution.py:60
  320.3 141.2 %all-gather.9.cloned.1.call-done = bf16[1024,6656]{1,0:T(8,128)(2,1)} async-done(((bf16[128,6656]{1,0:T(8,128)(2,1)}), bf16[1024,6656]{1,0:T(8,128)(2,1)}) %all-gather.9.cloned.1.call-update) | async-done | bytes 13631504 | tf_op jit(solution)/shard_map/all_gather | solution.py:62
  461.5 9.5 %convolution_convert_fusion = bf16[1024,256]{1,0:T(8,128)(2,1)S(1)} fusion(bf16[1024,6656]{1,0:T(8,128)(2,1)} %all-gather.9.cloned.1.call-done, bf16[6656,256]{1,0:T(8,128)(2,1)} %all-gather.11.cloned.1.call-done), kind=kOutput, calls=%fused_computation.29 | convolution fusion | flops 3489923072 | bytes 17563648 | tf_op jit(solution)/shard_map/dot_general | solution.py:61
  471.1 7.5 %gather_fusion = bf16[2048,256]{1,0:T(8,128)(2,1)S(1)} fusion(bf16[1025,256]{1,0:T(8,128)(2,1)S(1)} %concatenate.3, s32[2048]{0:T(1024)S(1)} %fusion.28), kind=kCustom, calls=%fused_computation | custom fusion | bytes 2105344 | tf_op jit(solution)/shard_map/gather | solution.py:80
  478.6 38.0 %all_to_all.12 = bf16[32,64,256]{2,1,0:T(8,128)(2,1)S(1)} all-to-all(bf16[32,64,256]{2,1,0:T(8,128)(2,1)S(1)} %bitcast.51), channel_id=1, replica_groups=mesh['dp'=32,'inner'=8] {'dp'}, dimensions={0} | all-to-all | bytes 2097152 | tf_op jit(solution)/shard_map/all_to_all | solution.py:81
  516.6 1.0 copy.33
  (47 shorter events, 4.7 us)
Async XLA Ops:
  6.5 51.8 %copy-start = (bf16[512,1664]{1,0:T(8,128)(2,1)S(1)}, bf16[512,1664]{1,0:T(8,128)(2,1)}, u32[]{:S(2)}) copy-start(bf16[512,1664]{1,0:T(8,128)(2,1)} %param.8) | copy-start | bytes 5111812
  6.5 116.6 %all-gather.13.cloned.1.call-start = ((), (), s32[]{:S(2)}) async-start(), calls=%async_computation.4 | async-start | bytes 3311616 | tf_op jit(solution)/shard_map/all_gather | solution.py:53
  30.8 206.1 %all-gather.7.cloned.1.call-start = ((), (), s32[]{:S(2)}) async-start(), calls=%async_computation.1 | async-start | bytes 12300288 | tf_op jit(solution)/shard_map/all_gather | solution.py:45
  57.6 262.8 %all-gather.11.cloned.1.call-start = ((), (), s32[]{:S(2)}) async-start(), calls=%async_computation.3 | async-start | bytes 3514368 | tf_op jit(solution)/shard_map/all_gather | solution.py:60
  58.3 403.2 %all-gather.9.cloned.1.call-start = ((), (), s32[]{:S(2)}) async-start(), calls=%async_computation.2 | async-start | bytes 15335424 | tf_op jit(solution)/shard_map/all_gather | solution.py:62
  59.2 177.7 %copy-start.4 = (f32[1664]{0:T(1024)S(1)}, f32[1664]{0:T(1024)}, u32[]{:S(2)}) copy-start(f32[1664]{0:T(1024)} %param.9) | copy-start | bytes 19972
  258.1 4.3 copy-start.1
  269.7 2.7 copy-start.3
  272.4 1.8 copy-start.2
Sparse Core Ops, SparseCore 0:
  31.0 92.1 all-gather.12
  125.9 111.0 all-gather.6
  239.8 80.5 all-gather.10
  322.0 139.5 all-gather.8
where the time goes:
time: 525 us; the launch traced here: 524 us
  waiting for transfers between devices  344 us (66%)
  blocking collectives  85.5 us (16%)
  matrix products  37.7 us (7%)
  local copies, waits for them, and re-layouts  27.6 us (5%)
  other arithmetic  15.8 us (3%)
  between operations  13.4 us (3%)
    all_gather x1, waiting for transfers between devices, local(): lax.all_gather(merged, 'inner', axis=0, tiled=True)  141 us
    all_gather x1, waiting for transfers between devices, local(): lax.all_gather(qkv_part, 'dp', axis=1, tiled=True)  108 us
    all_gather x1, waiting for transfers between devices, local(): lax.all_gather(out_part, 'dp', axis=1, tiled=True)  62 us
    all_to_all x1, blocking collectives, local(): lax.all_to_all(outgoing, 'dp', split_axis=0, concat_axis=0, tiled=True)  38 us
    all_gather x1, waiting for transfers between devices, local(): merge_full = lax.all_gather(merge_weight, 'dp', axis=0, tiled=True)  32 us
    all_gather x1, blocking collectives, local(): qkv_part = lax.all_gather(qkv_weight, 'inner', axis=2, tiled=True)  24 us
    all_gather x1, blocking collectives, local(): out_part = lax.all_gather(out_weight, 'inner', axis=0, tiled=True)  23.5 us
    dot_general x1, matrix products, local(): jnp.einsum('td,cdh->cth', normed, lax.all_gather(qkv_part, 'dp', axis=1,...  12.2 us
  transfers between devices with their start and end apart: 4, of which 4 were waited for; matrix products, arithmetic and copies ran while one was open for 12% of the time, Pallas kernels for 0%

commit v1 on v0

--- a/solution.py
+++ b/solution.py
@@ -58,10 +58,15 @@
     live = local_segment.reshape(-1, 4)[:, 0] >= 0
     merged = jnp.where(live[:, None], layer_norm(quad_rows, merge_gain), 0.0).astype(jnp.bfloat16)
     merge_full = lax.all_gather(merge_weight, "dp", axis=0, tiled=True)
+
+    def perform_slots_now(dev_axis, panel):
+        current_value = lax.axis_size(dev_axis)
+        later = jnp.stack([panel] * current_value)
+        res = lax.all_to_all(later, dev_axis, 0, 0)
+        return jnp.concatenate(res, 0)
+
     features = jnp.dot(
-        lax.all_gather(merged, "inner", axis=0, tiled=True),
-        merge_full,
-        preferred_element_type=jnp.float32,
+        perform_slots_now("inner", merged), merge_full, preferred_element_type=jnp.float32
     ).astype(jnp.bfloat16)
     n_dp = lax.axis_size("dp")
     group_rows = features.shape[0]

time: 525 us -> 550 us (1.048)
  the two profiles are of different devices: /device:TPU:1 before, /device:TPU:30 now
where the time goes in v1:
time: 550 us; the launch traced here: 549 us
  waiting for transfers between devices  347 us (63%)
  blocking collectives  94.6 us (17%)
  matrix products  37.5 us (7%)
  local copies, waits for them, and re-layouts  35.3 us (6%)
  other arithmetic  15.6 us (3%)
  between operations  13.3 us (2%)
  starting transfers between devices  5.88 us (1%)
    all_gather x1, waiting for transfers between devices, local(): merge_full = lax.all_gather(merge_weight, 'dp', axis=0, tiled=True)  185 us
    all_gather x1, waiting for transfers between devices, local(): lax.all_gather(qkv_part, 'dp', axis=1, tiled=True)  108 us
    all_gather x1, waiting for transfers between devices, local(): lax.all_gather(out_part, 'dp', axis=1, tiled=True)  48.7 us
    all_to_all x1, blocking collectives, local(): lax.all_to_all(outgoing, 'dp', split_axis=0, concat_axis=0, tiled=True)  36.2 us
    all_gather x1, blocking collectives, local(): qkv_part = lax.all_gather(qkv_weight, 'inner', axis=2, tiled=True)  29.9 us
    all_gather x1, blocking collectives, local(): out_part = lax.all_gather(out_weight, 'inner', axis=0, tiled=True)  28.6 us
    dot_general x1, matrix products, local(): jnp.einsum('td,cdh->cth', normed, lax.all_gather(qkv_part, 'dp', axis=1,...  12.2 us
  transfers between devices with their start and end apart: 4, of which 4 were waited for; matrix products, arithmetic and copies ran while one was open for 5% of the time, Pallas kernels for 0%

profile of v1, /device:TPU:30, one launch (start us, length us, event | category | flops | bytes accessed | tf_op | source)
XLA Modules:
  0.0 549.3 jit_solution(15806895018662957013)
XLA Ops:
  6.5 28.6 %all-gather = bf16[8,104,52]{1,2,0:T(8,128)(2,1)S(1)} all-gather(bf16[1,104,52]{1,2,0:T(8,128)(2,1)} %bitcast.62), channel_id=1, replica_groups=mesh['dp'=32,'inner'=8] {'inner'}, dimensions={0}, use_global_device_ids=true | all-gather | bytes 97344 | tf_op jit(solution)/shard_map/all_gather | solution.py:50
  36.9 29.9 %all_gather.15 = bf16[3,52,832]{1,0,2:T(4,128)(2,1)S(1)} all-gather(bf16[3,52,104]{1,0,2:T(4,128)(2,1)S(1)} %copy.18), channel_id=1, replica_groups=mesh['dp'=32,'inner'=8] {'inner'}, dimensions={2}, use_global_device_ids=true | all-gather | bytes 292032 | tf_op jit(solution)/shard_map/all_gather | solution.py:41
  66.8 1.7 copy.19
  71.4 48.7 %all-gather.10.cloned.1.call-done = bf16[32,52,832]{2,1,0:T(8,128)(2,1)} async-done(((bf16[1,52,832]{2,1,0:T(8,128)(2,1)}), bf16[32,52,832]{2,1,0:T(8,128)(2,1)}) %all-gather.10.cloned.1.call-update) | async-done | bytes 2768912 | tf_op jit(solution)/shard_map/all_gather | solution.py:53
  120.0 5.7 %reshape.151 = bf16[1664,832]{1,0:T(8,128)(2,1)} reshape(bf16[32,52,832]{2,1,0:T(8,128)(2,1)} %all-gather.10.cloned.1.call-done) | data formatting | bytes 5537792
  125.7 108.1 %all-gather.6.cloned.1.call-done = bf16[3,1664,832]{2,0,1:T(4,128)(2,1)} async-done(((bf16[3,52,832]{2,0,1:T(4,128)(2,1)}), bf16[3,1664,832]{2,0,1:T(4,128)(2,1)}) %all-gather.6.cloned.1.call-update) | async-done | bytes 8306704 | tf_op jit(solution)/shard_map/all_gather | solution.py:45
  233.8 12.2 %convert_bitcast_fusion = bf16[3,512,832]{1,2,0:T(8,128)(2,1)S(1)} fusion(bf16[3,1664,832]{2,0,1:T(4,128)(2,1)} %all-gather.6.cloned.1.call-done, bf16[512,1664]{1,0:T(8,128)(2,1)S(1)} %copy-done, f32[1664]{0:T(1024)S(1)} %copy-done.4, f32[512]{0:T(512)S(1)} %add_rsqrt_fusion, f32[512]{0:T(512)S(1)} %broadcast_multiply_fusion), kind=kOutput, calls=%fused_computation.23 | convolution fusion | flops 4258562048 | bytes 12577280 | tf_op jit(solution)/shard_map/td,cdh->cth/dot_general | solution.py:42
  246.0 1.1 fusion.33
  247.1 7.6 %fusion.34 = (f32[8,512]{1,0:T(8,128)S(1)}, f32[8,512,512]{1,2,0:T(8,128)}) fusion(pred[512,512]{0,1:T(8,128)(4,1)} %broadcast_compare_fusion, bf16[512,8,104]{0,2,1:T(8,128)(2,1)} %bitcast.55, bf16[512,8,104]{0,2,1:T(8,128)(2,1)S(1)} %bitcast.54), kind=kOutput, calls=%fused_computation.54 | convolution fusion | flops 444596736 | bytes 10371072 | tf_op jit(solution)/shard_map/sub | solution.py:24
  254.8 4.3 fusion.20
  259.1 3.8 fusion.35
  263.4 3.1 reshape.128
  266.5 2.4 multiply_reduce_fusion
  269.2 1.8 select_convert_fusion
  271.0 7.5 %stack.2 = bf16[8,128,6656]{2,1,0:T(8,128)(2,1)} broadcast(bf16[128,6656]{1,0:T(8,128)(2,1)} %select_convert_fusion), dimensions={1,2} | broadcast | bytes 15335424 | tf_op jit(solution)/shard_map/stack | solution.py:64
  278.4 5.8 %all-to-all-start = ((bf16[8,128,6656]{2,1,0:T(8,128)(2,1)}), bf16[8,128,6656]{2,1,0:T(8,128)(2,1)}, u32[]{:S(2)}, u32[]{:S(2)}) async-start(bf16[8,128,6656]{2,1,0:T(8,128)(2,1)} %stack.2), calls=%async_computation | async-start | bytes 27262976 | tf_op jit(solution)/shard_map/all_to_all | solution.py:65
  285.0 9.0 %reduce-window.6 = s32[32,8,128]{2,1,0:T(8,128)S(1)} reduce-window(s32[32,8,128]{2,1,0:T(8,128)S(1)} %fusion.26, s32[]{:T(128)} %constant.18.clone.1), window={size=1x1x128 pad=0_0x0_0x127_0}, to_apply=%region_8.9 | reduce-window | flops 4161536 | bytes 262148 | tf_op jit(solution)/shard_map/reduce-window
  294.6 4.3 scatter_custom_fusion
  298.9 185.3 %all-gather.8.cloned.1.call-done = bf16[6656,256]{1,0:T(8,128)(2,1)} async-done(((bf16[208,256]{1,0:T(8,128)(2,1)}), bf16[6656,256]{1,0:T(8,128)(2,1)}) %all-gather.8.cloned.1.call-update) | async-done | bytes 3407888 | tf_op jit(solution)/shard_map/all_gather | solution.py:60
  484.2 4.2 all-to-all-done
  488.5 9.5 %convolution_convert_fusion = bf16[1024,256]{1,0:T(8,128)(2,1)S(1)} fusion(bf16[1024,6656]{1,0:T(8,128)(2,1)} %bitcast.10, bf16[6656,256]{1,0:T(8,128)(2,1)} %all-gather.8.cloned.1.call-done), kind=kOutput, calls=%fused_computation.29 | convolution fusion | flops 3489923072 | bytes 17563648 | tf_op jit(solution)/shard_map/dot_general | solution.py:68
  498.1 7.5 %gather_fusion = bf16[2048,256]{1,0:T(8,128)(2,1)S(1)} fusion(bf16[1025,256]{1,0:T(8,128)(2,1)S(1)} %concatenate.3, s32[2048]{0:T(1024)S(1)} %fusion.28), kind=kCustom, calls=%fused_computation | custom fusion | bytes 2105344 | tf_op jit(solution)/shard_map/gather | solution.py:85
  505.6 36.2 %all_to_all.17 = bf16[32,64,256]{2,1,0:T(8,128)(2,1)S(1)} all-to-all(bf16[32,64,256]{2,1,0:T(8,128)(2,1)S(1)} %bitcast.52), channel_id=1, replica_groups=mesh['dp'=32,'inner'=8] {'dp'}, dimensions={0} | all-to-all | bytes 2097152 | tf_op jit(solution)/shard_map/all_to_all | solution.py:86
  541.8 1.0 copy.33
  (47 shorter events, 6.5 us)
Async XLA Ops:
  6.5 63.0 %copy-start = (bf16[512,1664]{1,0:T(8,128)(2,1)S(1)}, bf16[512,1664]{1,0:T(8,128)(2,1)}, u32[]{:S(2)}) copy-start(bf16[512,1664]{1,0:T(8,128)(2,1)} %param.8) | copy-start | bytes 5111812
  6.5 113.5 %all-gather.10.cloned.1.call-start = ((), (), s32[]{:S(2)}) async-start(), calls=%async_computation.4 | async-start | bytes 3311616 | tf_op jit(solution)/shard_map/all_gather | solution.py:53
  35.9 197.9 %all-gather.6.cloned.1.call-start = ((), (), s32[]{:S(2)}) async-start(), calls=%async_computation.2 | async-start | bytes 12300288 | tf_op jit(solution)/shard_map/all_gather | solution.py:45
  70.4 163.4 %copy-start.4 = (f32[1664]{0:T(1024)S(1)}, f32[1664]{0:T(1024)}, u32[]{:S(2)}) copy-start(f32[1664]{0:T(1024)} %param.9) | copy-start | bytes 19972
  254.8 4.3 copy-start.1
  266.5 2.7 copy-start.3
  278.4 6.6 %copy-start.2 = (s32[1024,1]{0,1:T(1,128)S(1)}, s32[1024,1]{0,1:T(1,128)}, u32[]{:S(2)}) copy-start(s32[1024,1]{0,1:T(1,128)} %param.15) | copy-start | bytes 12292
  278.4 210.0 %all-to-all-start = ((bf16[8,128,6656]{2,1,0:T(8,128)(2,1)}), bf16[8,128,6656]{2,1,0:T(8,128)(2,1)}, u32[]{:S(2)}, u32[]{:S(2)}) async-start(bf16[8,128,6656]{2,1,0:T(8,128)(2,1)} %stack.2), calls=%async_computation | async-start | bytes 27262976 | tf_op jit(solution)/shard_map/all_to_all | solution.py:65
  284.3 200.0 %all-gather.8.cloned.1.call-start = ((), (), s32[]{:S(2)}) async-start(), calls=%async_computation.3 | async-start | bytes 3514368 | tf_op jit(solution)/shard_map/all_gather | solution.py:60
Sparse Core Ops, SparseCore 0:
  36.0 83.9 all-gather.9
  122.8 111.0 all-gather.5
  287.8 196.3 all-gather.7
